TPU v7x, 256 devices: a whole 4x4x8 slice. The times are simulated.
256 devices in a mesh: req: 32 (over z_hi, x, y), cand: 8 (over z_lo, core).
Axes of the slice: x: 4, y: 4, z: 8 (z_hi: 2, z_lo: 4; z = z_hi * 4 + z_lo), core: 2. Of those that a mesh axis runs over, the one named last changes fastest.
Arguments:
- item_table: bfloat16 [32, 8, 256, 1024], P('req', 'cand'), may hold values from -25 to 25
- picked_items: int32 [32, 8, 1024], P('req', 'cand'), may hold values from 0 to 255
- destination: int32 [32, 8, 1024], P('req', 'cand'), may hold values from 0 to 31, as said below
- slot_index: int32 [32, 8, 1024], P('req', 'cand'), may hold values from 0 to 1023, as said below
- history_cache: bfloat16 [32, 8, 128, 2048], P('req', 'cand'), may hold values from -6 to 6
- history_length: int32 [32, 8], P('req'), may hold values from 16 to 128
- input_weight: bfloat16 [1024, 4096], replicated, may hold values from -0.1875 to 0.1875
- output_weight: bfloat16 [1024, 1024], replicated, may hold values from -0.1875 to 0.1875
Outputs:
- cand_out: bfloat16 [32, 8, 1024, 1024], P('req', 'cand')
Inputs may be any that keep to these rules, and one draw needn't show every extreme that they name: Each device sends exactly 1024 rows, and within each index of cand every device receives exactly 1024; no device sends more than 64 rows to one destination, and within each index of cand some device sends exactly 64 to one destination. `slot_index`: the rows that reach one device fill each of its 1024 slots exactly once.
All inputs are finite; a program needn't handle non-finite values.
Results may differ from a plain program's by a relative error of at most 0.005.
Values may be sent and summed in bfloat16 or wider, within the bound.
No kernel may reach another device: no remote copies, remote signals or barrier semaphores. Data moves between devices by JAX's collectives and lax.ppermute only.
A program may use at most 128 MiB of HBM per device.

v0:
```python
import math
import jax
import jax.numpy as jnp
from jax import lax
from jax.sharding import Mesh
from jax.sharding import PartitionSpec as P

HEADS = 8
HALVES = 2
epsilon = 1e-06


def layer_norm(values):
    average = jnp.mean(values, axis=-1, keepdims=True)
    centred = values - average
    variance = jnp.mean(centred * centred, axis=-1, keepdims=True)
    return centred * lax.rsqrt(variance + epsilon)


def attend(queries, cache_rows, lengths, head_count, score_scale):
    count_req, history_span, doubled = cache_rows.shape
    feature = doubled // 2
    head_width = feature // head_count
    keys = cache_rows[:, :, :feature].reshape(count_req, history_span, head_count, head_width)
    values = cache_rows[:, :, feature:].reshape(count_req, history_span, head_count, head_width)
    scores = (
        jnp.einsum("bihe,bjhe->bhij", queries, keys, preferred_element_type=jnp.float32)
        * score_scale
    )
    positions = jnp.arange(history_span, dtype=jnp.int32)
    valid = (positions[None, :] < lengths[:, None]).astype(jnp.float32)
    length_plus = lengths.astype(jnp.float32) + 1.0
    weights = (
        jax.nn.silu(scores) / length_plus[:, None, None, None] * valid[:, None, None, :]
    ).astype(jnp.bfloat16)
    return jnp.einsum("bhij,bjhe->bihe", weights, values, preferred_element_type=jnp.float32)


def ranks(targets, sources):
    count = targets.shape[0]
    one_hot = targets[:, None] == jnp.arange(sources, dtype=jnp.int32)[None, :]
    rows = jnp.arange(count, dtype=jnp.int32)
    lower = (rows[None, :] < rows[:, None]).astype(jnp.bfloat16)
    earlier = jnp.dot(lower, one_hot.astype(jnp.bfloat16), preferred_element_type=jnp.float32)
    return jnp.sum(jnp.where(one_hot, earlier, 0.0), axis=1).astype(jnp.int32)


def block_plan(ints, half, n_half, per_pair, sources):
    picks, targets, places = (ints[0], ints[1], ints[2])
    within = ranks(targets, sources)
    keep = targets // n_half == half
    position = jnp.where(keep, targets % n_half * per_pair + within, -1)
    spots = jnp.arange(n_half * per_pair, dtype=jnp.int32)
    hit = position[None, :] == spots[:, None]
    row = jnp.sum(jnp.where(hit, picks[None, :], 0), axis=1)
    slot = jnp.sum(jnp.where(hit, places[None, :] + 1, 0), axis=1) - 1
    return (row.reshape(n_half, per_pair), slot.reshape(n_half, per_pair))


def shards(
    item_table,
    picked_items,
    destination,
    slot_index,
    history_cache,
    history_length,
    input_weight,
    output_weight,
):
    n_half = lax.axis_size("xy")
    sources = HALVES * n_half
    half = lax.axis_index("zh")
    item_rows = item_table[0, 0]
    ints = jnp.stack([picked_items[0, 0], destination[0, 0], slot_index[0, 0]])
    slot_count = ints.shape[1]
    feature = item_rows.shape[1]
    per_pair = 2 * slot_count // sources
    swap = [(0, 1), (1, 0)]
    other_rows = lax.ppermute(item_rows, "zh", swap)
    other_ints = lax.ppermute(ints, "zh", swap)
    own_row, own_slot = block_plan(ints, half, n_half, per_pair, sources)
    far_row, far_slot = block_plan(other_ints, half, n_half, per_pair, sources)
    own_data = jnp.take(item_rows, own_row.reshape(-1), axis=0).reshape(n_half, per_pair, feature)
    far_data = jnp.take(other_rows, far_row.reshape(-1), axis=0).reshape(n_half, per_pair, feature)
    slots = jnp.concatenate([own_slot, far_slot], axis=1)
    capacity = 2 * per_pair
    radix = 32
    high = jnp.floor_divide(slots, radix)
    low = slots - high * radix
    tag_row = jnp.zeros((n_half, 8, feature), jnp.float32)
    tag_row = tag_row.at[:, 0, :capacity].set(high.astype(jnp.float32))
    tag_row = tag_row.at[:, 0, capacity : 2 * capacity].set(low.astype(jnp.float32))
    outgoing = jnp.concatenate([own_data, far_data, tag_row.astype(jnp.bfloat16)], axis=1)
    arrived = lax.all_to_all(outgoing, "xy", split_axis=0, concat_axis=0, tiled=True)
    arrived_rows = arrived[:, :capacity].reshape(n_half * capacity, feature)
    tags = (
        arrived[:, capacity, :capacity].astype(jnp.int32) * radix
        + arrived[:, capacity, capacity : 2 * capacity].astype(jnp.int32)
    ).reshape(-1)
    slot_ids = jnp.arange(slot_count, dtype=jnp.int32)
    order = jnp.arange(n_half * capacity, dtype=jnp.int32)
    fill = jnp.sum(jnp.where(tags[None, :] == slot_ids[:, None], order[None, :], 0), axis=1)
    arranged = jnp.take(arrived_rows, fill, axis=0)
    lengths = history_length[0]
    members = lengths.shape[0]
    per_request = slot_count // members
    head_count = HEADS
    head_width = feature // head_count
    score_scale = 1.0 / math.sqrt(head_width)
    as_float = arranged.astype(jnp.float32)
    normed_in = layer_norm(as_float).astype(jnp.bfloat16)
    projected = jax.nn.silu(
        jnp.dot(normed_in, input_weight, preferred_element_type=jnp.float32)
    ).astype(jnp.bfloat16)
    quarters = projected.reshape(members, per_request, 4, head_count, head_width)
    gate_u = projected[:, :feature]
    own_values = quarters[:, :, 1]
    queries = quarters[:, :, 2]
    own_keys = quarters[:, :, 3]
    length_plus = lengths.astype(jnp.float32) + 1.0
    own_scores = (
        jnp.einsum("bihe,bihe->bih", queries, own_keys, preferred_element_type=jnp.float32)
        * score_scale
    )
    own_weight = jax.nn.silu(own_scores) / length_plus[:, None, None]
    own_term = own_weight[..., None] * own_values.astype(jnp.float32)
    found = attend(
        queries,
        lax.all_gather(history_cache, "cand", axis=1, tiled=True)[0],
        lengths,
        head_count,
        score_scale,
    )
    attended = (found + own_term).reshape(slot_count, feature)
    normed_out = layer_norm(attended)
    gated = (normed_out * gate_u.astype(jnp.float32)).astype(jnp.bfloat16)
    mixed = as_float + jnp.dot(gated, output_weight, preferred_element_type=jnp.float32)
    return mixed.astype(jnp.bfloat16)[None, None]


def solution(mesh):
    n_req, n_cand = mesh.devices.shape
    devices = mesh.devices.reshape(HALVES, n_req // HALVES, n_cand)
    split = Mesh(devices, ("zh", "xy", "cand"))
    req = ("zh", "xy")
    in_specs = (
        P(req, "cand", None, None),
        P(req, "cand", None),
        P(req, "cand", None),
        P(req, "cand", None),
        P(req, "cand", None, None),
        P(req, None),
        P(),
        P(),
    )
    out_specs = P(req, "cand", None, None)
    return jax.shard_map(
        shards, mesh=split, in_specs=in_specs, out_specs=out_specs, check_vma=False
    )
```

profile of v0, /device:TPU:220, one launch (start us, length us, event | category | flops | bytes accessed | tf_op | source)
XLA Modules:
  0.0 224.5 jit_solution(4971782553543339096)
XLA Ops:
  8.1 5.4 %collective-permute-start = (bf16[256,1024]{1,0:T(8,128)(2,1)}, bf16[256,1024]{1,0:T(8,128)(2,1)S(1)}, u32[]{:S(2)}, u32[]{:S(2)}) collective-permute-start(bf16[256,1024]{1,0:T(8,128)(2,1)} %bitcast.70), channel_id=1, source_target_pairs={{0,128},{128,0},{1,129},{129,1},{2,130},{130,2},{3,131},{131,3},{4... | collective-permute-start | bytes 1572872 | tf_op jit(solution)/shard_map/ppermute | solution.py:79
  18.1 5.3 %gather_fusion.1 = bf16[1024,1024]{1,0:T(8,128)(2,1)} fusion(bf16[256,1024]{1,0:T(8,128)(2,1)S(1)} %bitcast.71, s32[1024]{0:T(1024)S(1)} %get-tuple-element.49), kind=kCustom, calls=%fused_computation.clone | custom fusion | bytes 4198400 | tf_op jit(solution)/shard_map/jit(_take)/gather | solution.py:83
  23.5 3.2 %broadcast_select_fusion.1 = bf16[1024,1024]{1,0:T(8,128)(2,1)} fusion(bf16[1024,1024]{1,0:T(8,128)(2,1)} %gather_fusion.1, pred[1024]{0:T(1024)(128)(4,1)S(1)} %compare_and_fusion.1), kind=kLoop, calls=%fused_computation.44 | loop fusion | flops 1048576 | bytes 4195328 | tf_op jit(solution)/shard_map/jit(_take)/select_n | solution.py:83
  33.8 3.6 %collective-permute-done = bf16[256,1024]{1,0:T(8,128)(2,1)S(1)} collective-permute-done((bf16[256,1024]{1,0:T(8,128)(2,1)}, bf16[256,1024]{1,0:T(8,128)(2,1)S(1)}, u32[]{:S(2)}, u32[]{:S(2)}) %collective-permute-start) | collective-permute-done | bytes 524320 | tf_op jit(solution)/shard_map/ppermute | solution.py:79
  37.3 5.3 %gather_fusion.2 = bf16[1024,1024]{1,0:T(8,128)(2,1)} fusion(bf16[256,1024]{1,0:T(8,128)(2,1)S(1)} %collective-permute-done, s32[1024]{0:T(1024)S(1)} %fusion.44), kind=kCustom, calls=%fused_computation.1.clone | custom fusion | bytes 4198400 | tf_op jit(solution)/shard_map/jit(_take)/gather | solution.py:84
  44.9 2.3 %pad_maximum_fusion = bf16[16,136,1024]{2,1,0:T(8,128)(2,1)} fusion(bf16[16,8,1024]{2,1,0:T(8,128)(2,1)S(1)} %scatter.9, bf16[16,64,1024]{2,1,0:T(8,128)(2,1)S(1)} %bitcast.77, bf16[16,64,1024]{2,1,0:T(8,128)(2,1)S(1)} %bitcast.76), kind=kLoop, calls=%fused_computation.11 | loop fusion | flops 13369344 | bytes 8912896 | tf_op jit(solution)/shard_map/concatenate | solution.py:93
  47.2 7.2 %all-to-all-start = ((bf16[16,136,1024]{2,1,0:T(8,128)(2,1)}), bf16[16,136,1024]{2,1,0:T(8,128)(2,1)}, u32[]{:S(2)}, u32[]{:S(2)}) async-start(bf16[16,136,1024]{2,1,0:T(8,128)(2,1)} %pad_maximum_fusion), calls=%async_computation | async-start | bytes 8912896 | tf_op jit(solution)/shard_map/all_to_all | solution.py:94
  55.3 67.1 %all-to-all-done = bf16[16,136,1024]{2,1,0:T(8,128)(2,1)} async-done(((bf16[16,136,1024]{2,1,0:T(8,128)(2,1)}), bf16[16,136,1024]{2,1,0:T(8,128)(2,1)}, u32[]{:S(2)}, u32[]{:S(2)}) %all-to-all-start) | async-done | bytes 4456480 | tf_op jit(solution)/shard_map/all_to_all | solution.py:94
  122.3 4.8 %slice.113 = bf16[16,128,1024]{2,1,0:T(8,128)(2,1)} slice(bf16[16,136,1024]{2,1,0:T(8,128)(2,1)} %all-to-all-done), slice={[0:16], [0:128], [0:1024]} | slice | bytes 8388608 | tf_op jit(solution)/shard_map/slice | solution.py:95
  128.8 8.9 %gather_fusion = bf16[1024,1024]{1,0:T(8,128)(2,1)} fusion(bf16[2048,1024]{1,0:T(8,128)(2,1)} %bitcast.72, s32[1024]{0:T(1024)S(1)} %broadcast_clamp_fusion), kind=kCustom, calls=%fused_computation.2 | custom fusion | bytes 4198400 | tf_op jit(solution)/shard_map/jit(_take)/gather | solution.py:103
  137.8 2.3 %convert_reduce_fusion = f32[1024]{0:T(1024)S(1)} fusion(bf16[1024,1024]{1,0:T(8,128)(2,1)} %gather_fusion, pred[1024]{0:T(1024)(128)(4,1)S(1)} %compare_and_fusion.2), kind=kLoop, calls=%fused_computation.8 | loop fusion | flops 3144704 | bytes 2102272 | tf_op jit(solution)/shard_map/reduce_sum | solution.py:14
  140.1 2.4 %fusion.2 = f32[1024]{0:T(1024)S(1)} fusion(f32[1024]{0:T(1024)S(1)} %broadcast_multiply_fusion.1, bf16[1024,1024]{1,0:T(8,128)(2,1)} %gather_fusion, pred[1024]{0:T(1024)(128)(4,1)S(1)} %compare_and_fusion.2), kind=kLoop, calls=%fused_computation.12 | loop fusion | flops 5241856 | bytes 2106368 | tf_op jit(solution)/shard_map/reduce_sum | solution.py:16
  142.6 15.8 %multiply_convert_fusion = bf16[1024,4096]{1,0:T(8,128)(2,1)} fusion(bf16[1024,4096]{1,0:T(8,128)(2,1)} %param.20, f32[1024]{0:T(1024)S(1)} %add_rsqrt_fusion, f32[1024]{0:T(1024)S(1)} %broadcast_multiply_fusion.1, bf16[1024,1024]{1,0:T(8,128)(2,1)S(1)} %copy-done.2, pred[1024]{0:T(1024)(128)(4,1)S(1)} %compare_and_fusion.2), kind=kOutput, calls=%fused_computation.3 | convolution fusion | flops 8616148992 | bytes 18883584 | tf_op jit(solution)/shard_map/dot_general | solution.py:113
  158.4 9.4 %copy.38 = bf16[128,8,32,128]{3,2,1,0:T(8,128)(2,1)} copy(bf16[128,8,32,128]{3,1,2,0:T(8,128)(2,1)} %bitcast.78) | data formatting | bytes 16777216
  167.8 4.8 %fusion.49 = (bf16[8,128,1,8,128]{4,3,2,1,0:T(8,128)(2,1)}, bf16[8,128,1,8,128]{4,3,2,1,0:T(8,128)(2,1)}) fusion(bf16[8,128,4,8,128]{4,3,2,1,0:T(8,128)(2,1)} %bitcast.73), kind=kLoop, calls=%fused_computation.115 | loop fusion | bytes 8388608 | tf_op jit(solution)/shard_map/slice | solution.py:118
  172.6 4.1 %copy.37 = bf16[8,128,1,8,128]{1,4,3,0,2:T(8,128)(2,1)} copy(bf16[8,128,1,8,128]{4,3,2,1,0:T(8,128)(2,1)} %get-tuple-element.37) | data formatting | bytes 4194304
  176.7 2.1 fusion.23
  178.9 4.2 %multiply_reduce_fusion = f32[8,128,8]{2,1,0:T(8,128)S(1)} fusion(f32[8,128,8,128]{3,1,2,0:T(8,128)S(1)} %fusion.23, bf16[8,128,4,8,128]{4,3,2,1,0:T(8,128)(2,1)} %bitcast.74), kind=kLoop, calls=%fused_computation.21 | loop fusion | flops 3137536 | bytes 6324224
  183.3 6.5 %copy.26 = bf16[1,8,128,2048]{2,3,1,0:T(8,128)(2,1)} copy(bf16[1,8,128,2048]{3,2,0,1:T(8,128)(2,1)} %all-gather.2.cloned.1.call-done) | data formatting | bytes 8388608 | tf_op jit(solution)/shard_map/all_gather | solution.py:129
  189.8 4.6 %fusion.50 = (bf16[8,128,1024]{1,2,0:T(8,128)(2,1)}, bf16[8,128,1024]{1,2,0:T(8,128)(2,1)}) fusion(bf16[8,128,2048]{1,2,0:T(8,128)(2,1)} %bitcast.75), kind=kLoop, calls=%fused_computation.116 | loop fusion | bytes 8388608 | tf_op jit(solution)/shard_map/slice | solution.py:24
  194.4 8.2 %fusion.52 = (f32[8,128]{1,0:T(8,128)S(1)}, f32[8,128,8,128]{1,3,2,0:T(8,128)}) fusion(bf16[8,128,1,8,128]{1,4,3,0,2:T(8,128)(2,1)} %copy.37, f32[8,128,8]{1,2,0:T(8,128)S(1)} %multiply_divide_fusion, bf16[8,128,8,128]{1,3,2,0:T(8,128)(2,1)} %bitcast.81, bf16[8,128,8,128]{1,3,2,0:T(8,128)(2,1)} %bitcast.80, f32[8,128]{1,0:T(8,128)S(1)} %fusion.41, ...), kind=kOutput, calls=%fused_computation.118 | convolution fusion | flops 549452800 | bytes 12623904 | tf_op jit(solution)/shard_map/bhij,bjhe->bihe/dot_general | solution.py:36
  202.6 5.4 %copy.29 = f32[8,128,8,128]{3,2,1,0:T(8,128)} copy(f32[8,128,8,128]{1,3,2,0:T(8,128)} %get-tuple-element.48) | data formatting | bytes 8388608 | tf_op jit(solution)/shard_map/add | solution.py:134
  208.0 2.8 %multiply_reduce_fusion.1 = f32[8,128]{1,0:T(8,128)S(1)} fusion(f32[8,128,8,128]{1,3,2,0:T(8,128)} %get-tuple-element.48, f32[8,128]{1,0:T(8,128)S(1)} %get-tuple-element.44), kind=kLoop, calls=%fused_computation.22 | loop fusion | flops 3144704 | bytes 4202496 | tf_op jit(solution)/shard_map/reduce_sum | solution.py:16
  210.8 6.8 %fusion.13 = bf16[1,1,1024,1024]{3,2,1,0:T(8,128)(2,1)} fusion(bf16[1024,1024]{1,0:T(8,128)(2,1)S(1)} %copy-done, f32[128,8,8,128]{3,2,1,0:T(8,128)} %bitcast.79, bf16[1024,4096]{1,0:T(8,128)(2,1)} %multiply_convert_fusion, f32[1024]{0:T(1024)S(1)} %rsqrt_bitcast_fusion, f32[1024]{0:T(1024)S(1)} %get-tuple-element.43, bf16[1024,1024]{1,0:T(8,128)(2,1)S(1)} %copy-done.3, ...), kind=kOutput, calls=%fused_computation.34 | convolution fusion | flops 2156920832 | bytes 12592128 | tf_op jit(solution)/shard_map/dot_general | solution.py:137
  (57 shorter events, 18.2 us)
Async XLA Ops:
  6.5 204.3 %copy-start = (bf16[1024,1024]{1,0:T(8,128)(2,1)S(1)}, bf16[1024,1024]{1,0:T(8,128)(2,1)}, u32[]{:S(2)}) copy-start(bf16[1024,1024]{1,0:T(8,128)(2,1)} %param.21) | copy-start | bytes 6291460
  6.5 11.6 %copy-start.1 = (bf16[1,1,256,1024]{3,2,1,0:T(8,128)(2,1)S(1)}, bf16[1,1,256,1024]{3,2,1,0:T(8,128)(2,1)}, u32[]{:S(2)}) copy-start(bf16[1,1,256,1024]{3,2,1,0:T(8,128)(2,1)} %param.14) | copy-start | bytes 1572868
  7.4 20.6 %collective-permute-start.1 = (s32[3,1024]{1,0:T(4,128)S(1)}, s32[3,1024]{1,0:T(4,128)S(1)}, u32[]{:S(2)}, u32[]{:S(2)}) collective-permute-start(s32[3,1024]{1,0:T(4,128)S(1)} %pad_add_fusion), channel_id=1, source_target_pairs={{0,128},{128,0},{1,129},{129,1},{2,130},{130,2},{3,131},{131,3},{4... | collective-permute-start | bytes 36872 | tf_op jit(solution)/shard_map/ppermute | solution.py:80
  8.1 29.3 %collective-permute-start = (bf16[256,1024]{1,0:T(8,128)(2,1)}, bf16[256,1024]{1,0:T(8,128)(2,1)S(1)}, u32[]{:S(2)}, u32[]{:S(2)}) collective-permute-start(bf16[256,1024]{1,0:T(8,128)(2,1)} %bitcast.70), channel_id=1, source_target_pairs={{0,128},{128,0},{1,129},{129,1},{2,130},{130,2},{3,131},{131,3},{4... | collective-permute-start | bytes 1572872 | tf_op jit(solution)/shard_map/ppermute | solution.py:79
  23.5 3.2 %copy-start.6 = (s32[3]{0:T(128)S(1)}, s32[3]{0:T(128)}, u32[]{:S(2)}) copy-start(s32[3]{0:T(128)} %constant.161.clone.1) | copy-start | bytes 40
  42.7 2.2 copy-start.4
  47.2 8.0 %copy-start.5 = (s32[1,8]{1,0:T(1,128)S(1)}, s32[1,8]{1,0:T(1,128)}, u32[]{:S(2)}) copy-start(s32[1,8]{1,0:T(1,128)} %param.19) | copy-start | bytes 100
  47.2 75.1 %all-to-all-start = ((bf16[16,136,1024]{2,1,0:T(8,128)(2,1)}), bf16[16,136,1024]{2,1,0:T(8,128)(2,1)}, u32[]{:S(2)}, u32[]{:S(2)}) async-start(bf16[16,136,1024]{2,1,0:T(8,128)(2,1)} %pad_maximum_fusion), calls=%async_computation | async-start | bytes 8912896 | tf_op jit(solution)/shard_map/all_to_all | solution.py:94
  54.5 128.9 %all-gather.2.cloned.1.call-start = ((), (), s32[]{:S(2)}) async-start(), calls=%async_computation.1 | async-start | bytes 4718592 | tf_op jit(solution)/shard_map/all_gather | solution.py:129
  137.8 4.8 %copy-start.2 = (bf16[1024,1024]{1,0:T(8,128)(2,1)S(1)}, bf16[1024,1024]{1,0:T(8,128)(2,1)}, u32[]{:S(2)}) copy-start(bf16[1024,1024]{1,0:T(8,128)(2,1)} %gather_fusion) | copy-start | bytes 6291460
  208.0 2.9 %copy-start.3 = (bf16[1024,1024]{1,0:T(8,128)(2,1)S(1)}, bf16[1024,1024]{1,0:T(8,128)(2,1)}, u32[]{:S(2)}) copy-start(bf16[1024,1024]{1,0:T(8,128)(2,1)} %gather_fusion) | copy-start | bytes 6291460
Sparse Core Ops, SparseCore 0:
  57.0 52.5 all-gather.1
where the time goes:
time: 225 us; the launch traced here: 224 us
  waiting for transfers between devices  71.3 us (32%)
  local copies, waits for them, and re-layouts  61.9 us (28%)
  matrix products  32.6 us (14%)
  other arithmetic  31.7 us (14%)
  between operations  13.6 us (6%)
  starting transfers between devices  13.3 us (6%)
    all_to_all x1, waiting for transfers between devices, shards(): lax.all_to_all(outgoing, 'xy', split_axis=0, concat_axis=0, tiled=True)  67.1 us
    dot_general x1, matrix products, shards(): jnp.dot(normed_in, input_weight, preferred_element_type=jnp.float32)  15.8 us
    unnamed x16, local copies, waits for them, and re-layouts  13.8 us
    gather x1, local copies, waits for them, and re-layouts, shards(): arranged = jnp.take(arrived_rows, fill, axis=0)  8.92 us
    dot_general x1, matrix products, attend(): jnp.einsum('bhij,bjhe->bihe', weights, values, preferred_element_type=jnp...  8.22 us
    all_to_all x1, starting transfers between devices, shards(): lax.all_to_all(outgoing, 'xy', split_axis=0, concat_axis=0, tiled=True)  7.24 us
    dot_general x1, matrix products, shards(): jnp.dot(gated, output_weight, preferred_element_type=jnp.float32)  6.8 us
    all_gather x1, local copies, waits for them, and re-layouts, shards(): lax.all_gather(history_cache, 'cand', axis=1, tiled=True)[0]  6.47 us
  transfers between devices with their start and end apart: 4, of which 2 were waited for; matrix products, arithmetic and copies ran while one was open for 36% of the time, Pallas kernels for 0%

commit v1 on v0

--- a/solution.py
+++ b/solution.py
@@ -8,6 +8,10 @@
 HEADS = 8
 HALVES = 2
 epsilon = 1e-06
+point_marks = lambda body: jnp.concatenate(
+    lax.all_to_all(jnp.stack([body for _ in range(lax.axis_size("cand"))], axis=0), "cand", 0, 0),
+    axis=1,
+)
 
 
 def layer_norm(values):
@@ -124,13 +128,7 @@
     )
     own_weight = jax.nn.silu(own_scores) / length_plus[:, None, None]
     own_term = own_weight[..., None] * own_values.astype(jnp.float32)
-    found = attend(
-        queries,
-        lax.all_gather(history_cache, "cand", axis=1, tiled=True)[0],
-        lengths,
-        head_count,
-        score_scale,
-    )
+    found = attend(queries, point_marks(history_cache)[0], lengths, head_count, score_scale)
     attended = (found + own_term).reshape(slot_count, feature)
     normed_out = layer_norm(attended)
     gated = (normed_out * gate_u.astype(jnp.float32)).astype(jnp.bfloat16)

time: 225 us -> 245 us (1.089); the launches traced: 224 us -> 241 us
  waiting for transfers between devices: 71.3 us -> 101 us
  between operations: 13.6 us -> 0.25 us
  starting transfers between devices: 13.3 us -> 17.9 us
  local copies, waits for them, and re-layouts: 61.9 us -> 57.9 us
    all_to_all x0 -> x1, waiting for transfers between devices: none -> 29.6 us  [lax.all_to_all(jnp.stack([body for _ in range(lax.axis_size('cand'))], ax...]
    all_gather x1 -> x0, local copies, waits for them, and re-layouts: 6.47 us -> none  [shards(): lax.all_gather(history_cache, 'cand', axis=1, tiled=True)[0]]
    all_to_all x0 -> x1, starting transfers between devices: none -> 4.67 us  [lax.all_to_all(jnp.stack([body for _ in range(lax.axis_size('cand'))], ax...]
    another operation x1 -> x3, local copies, waits for them, and re-layouts: 0.59 us -> 3.37 us  [the longest x1 2.51 us: jnp.stack([body for _ in range(lax.axis_size('cand'))], axis=0)]
    unnamed x16 -> x18, local copies, waits for them, and re-layouts: 13.8 us -> 13.8 us
  transfers between devices with their start and end apart: 4 -> 4, of which waited for: 2 -> 3; matrix products, arithmetic and copies ran while one was open for 36% -> 34% of each run, Pallas kernels for 0% -> 0%
where the time goes in v1:
time: 245 us; the launch traced here: 241 us
  waiting for transfers between devices  101 us (41%)
  local copies, waits for them, and re-layouts  57.9 us (24%)
  matrix products  32.7 us (13%)
  other arithmetic  31.7 us (13%)
  starting transfers between devices  17.9 us (7%)
    all_to_all x1, waiting for transfers between devices, shards(): lax.all_to_all(outgoing, 'xy', split_axis=0, concat_axis=0, tiled=True)  67.5 us
    all_to_all x1, waiting for transfers between devices, lax.all_to_all(jnp.stack([body for _ in range(lax.axis_size('cand'))], ax...  29.6 us
    dot_general x1, matrix products, shards(): jnp.dot(normed_in, input_weight, preferred_element_type=jnp.float32)  15.8 us
    unnamed x18, local copies, waits for them, and re-layouts  13.8 us
    gather x1, local copies, waits for them, and re-layouts, shards(): arranged = jnp.take(arrived_rows, fill, axis=0)  8.74 us
    dot_general x1, matrix products, attend(): jnp.einsum('bhij,bjhe->bihe', weights, values, preferred_element_type=jnp...  8.23 us
    all_to_all x1, starting transfers between devices, shards(): lax.all_to_all(outgoing, 'xy', split_axis=0, concat_axis=0, tiled=True)  7.24 us
    dot_general x1, matrix products, shards(): jnp.dot(gated, output_weight, preferred_element_type=jnp.float32)  6.81 us
  transfers between devices with their start and end apart: 4, of which 3 were waited for; matrix products, arithmetic and copies ran while one was open for 34% of the time, Pallas kernels for 0%

profile of v1, /device:TPU:220, one launch (start us, length us, event | category | flops | bytes accessed | tf_op | source)
XLA Modules:
  0.0 241.1 jit_solution(1913103585225898523)
XLA Ops:
  1.5 5.4 %collective-permute-start = (bf16[256,1024]{1,0:T(8,128)(2,1)}, bf16[256,1024]{1,0:T(8,128)(2,1)S(1)}, u32[]{:S(2)}, u32[]{:S(2)}) collective-permute-start(bf16[256,1024]{1,0:T(8,128)(2,1)} %bitcast.70), channel_id=1, source_target_pairs={{0,128},{128,0},{1,129},{129,1},{2,130},{130,2},{3,131},{131,3},{4... | collective-permute-start | bytes 1572872 | tf_op jit(solution)/shard_map/ppermute | solution.py:83
  11.6 5.3 %gather_fusion.1 = bf16[1024,1024]{1,0:T(8,128)(2,1)} fusion(bf16[256,1024]{1,0:T(8,128)(2,1)S(1)} %bitcast.71, s32[1024]{0:T(1024)S(1)} %get-tuple-element.49), kind=kCustom, calls=%fused_computation.clone | custom fusion | bytes 4198400 | tf_op jit(solution)/shard_map/jit(_take)/gather | solution.py:87
  16.9 3.2 %broadcast_select_fusion.1 = bf16[1024,1024]{1,0:T(8,128)(2,1)} fusion(bf16[1024,1024]{1,0:T(8,128)(2,1)} %gather_fusion.1, pred[1024]{0:T(1024)(128)(4,1)S(1)} %compare_and_fusion.1), kind=kLoop, calls=%fused_computation.44 | loop fusion | flops 1048576 | bytes 4195328 | tf_op jit(solution)/shard_map/jit(_take)/select_n | solution.py:87
  27.2 3.6 %collective-permute-done = bf16[256,1024]{1,0:T(8,128)(2,1)S(1)} collective-permute-done((bf16[256,1024]{1,0:T(8,128)(2,1)}, bf16[256,1024]{1,0:T(8,128)(2,1)S(1)}, u32[]{:S(2)}, u32[]{:S(2)}) %collective-permute-start) | collective-permute-done | bytes 524320 | tf_op jit(solution)/shard_map/ppermute | solution.py:83
  30.8 5.3 %gather_fusion.2 = bf16[1024,1024]{1,0:T(8,128)(2,1)} fusion(bf16[256,1024]{1,0:T(8,128)(2,1)S(1)} %collective-permute-done, s32[1024]{0:T(1024)S(1)} %fusion.44), kind=kCustom, calls=%fused_computation.1.clone | custom fusion | bytes 4198400 | tf_op jit(solution)/shard_map/jit(_take)/gather | solution.py:88
  40.7 7.2 %all-to-all-start = ((bf16[16,136,1024]{2,1,0:T(8,128)(2,1)}), bf16[16,136,1024]{2,1,0:T(8,128)(2,1)}, u32[]{:S(2)}, u32[]{:S(2)}) async-start(bf16[16,136,1024]{2,1,0:T(8,128)(2,1)} %pad_maximum_fusion), calls=%async_computation | async-start | bytes 8912896 | tf_op jit(solution)/shard_map/all_to_all | solution.py:98
  48.3 67.5 %all-to-all-done = bf16[16,136,1024]{2,1,0:T(8,128)(2,1)} async-done(((bf16[16,136,1024]{2,1,0:T(8,128)(2,1)}), bf16[16,136,1024]{2,1,0:T(8,128)(2,1)}, u32[]{:S(2)}, u32[]{:S(2)}) %all-to-all-start) | async-done | bytes 4456480 | tf_op jit(solution)/shard_map/all_to_all | solution.py:98
  115.8 2.5 %stack.5 = bf16[8,1,1,128,2048]{3,4,2,1,0:T(8,128)(2,1)} broadcast(bf16[128,2048]{0,1:T(8,128)(2,1)S(1)} %copy.24), dimensions={3,4} | broadcast | bytes 4718592 | tf_op jit(solution)/shard_map/stack | solution.py:12
  118.3 4.7 %all-to-all-start.1 = ((bf16[8,1,1,128,2048]{3,4,2,1,0:T(8,128)(2,1)}), bf16[8,1,1,128,2048]{3,4,2,1,0:T(8,128)(2,1)}, u32[]{:S(2)}, u32[]{:S(2)}) async-start(bf16[8,1,1,128,2048]{3,4,2,1,0:T(8,128)(2,1)} %stack.5), calls=%async_computation.1 | async-start | bytes 8388608 | tf_op jit(solution)/shard_map/all_to_all | solution.py:12
  123.0 4.8 %slice.113 = bf16[16,128,1024]{2,1,0:T(8,128)(2,1)} slice(bf16[16,136,1024]{2,1,0:T(8,128)(2,1)} %all-to-all-done), slice={[0:16], [0:128], [0:1024]} | slice | bytes 8388608 | tf_op jit(solution)/shard_map/slice | solution.py:99
  129.5 8.7 %gather_fusion = bf16[1024,1024]{1,0:T(8,128)(2,1)} fusion(bf16[2048,1024]{1,0:T(8,128)(2,1)} %bitcast.72, s32[1024]{0:T(1024)S(1)} %broadcast_clamp_fusion), kind=kCustom, calls=%fused_computation.2 | custom fusion | bytes 4198400 | tf_op jit(solution)/shard_map/jit(_take)/gather | solution.py:107
  138.3 2.3 convert_reduce_fusion
  140.6 2.4 %fusion.2 = f32[1024]{0:T(1024)S(1)} fusion(f32[1024]{0:T(1024)S(1)} %broadcast_multiply_fusion.1, bf16[1024,1024]{1,0:T(8,128)(2,1)} %gather_fusion, pred[1024]{0:T(1024)(128)(4,1)S(1)} %compare_and_fusion.2), kind=kLoop, calls=%fused_computation.12 | loop fusion | flops 5241856 | bytes 2106368 | tf_op jit(solution)/shard_map/reduce_sum | solution.py:20
  143.1 15.8 %multiply_convert_fusion = bf16[1024,4096]{1,0:T(8,128)(2,1)} fusion(bf16[1024,4096]{1,0:T(8,128)(2,1)} %param.20, f32[1024]{0:T(1024)S(1)} %add_rsqrt_fusion, f32[1024]{0:T(1024)S(1)} %broadcast_multiply_fusion.1, bf16[1024,1024]{1,0:T(8,128)(2,1)S(1)} %copy-done.2, pred[1024]{0:T(1024)(128)(4,1)S(1)} %compare_and_fusion.2), kind=kOutput, calls=%fused_computation.3 | convolution fusion | flops 8616148992 | bytes 18883584 | tf_op jit(solution)/shard_map/dot_general | solution.py:117
  158.9 9.4 %copy.36 = bf16[128,8,32,128]{3,2,1,0:T(8,128)(2,1)} copy(bf16[128,8,32,128]{3,1,2,0:T(8,128)(2,1)} %bitcast.77) | data formatting | bytes 16777216
  168.3 4.6 %fusion.49 = (bf16[8,128,1,8,128]{4,3,2,1,0:T(8,128)(2,1)}, bf16[8,128,1,8,128]{4,3,2,1,0:T(8,128)(2,1)}) fusion(bf16[8,128,4,8,128]{4,3,2,1,0:T(8,128)(2,1)} %bitcast.73), kind=kLoop, calls=%fused_computation.115 | loop fusion | bytes 8388608 | tf_op jit(solution)/shard_map/slice | solution.py:122
  172.9 4.1 %copy.35 = bf16[8,128,1,8,128]{1,4,3,0,2:T(8,128)(2,1)} copy(bf16[8,128,1,8,128]{4,3,2,1,0:T(8,128)(2,1)} %get-tuple-element.37) | data formatting | bytes 4194304
  179.2 4.2 %multiply_reduce_fusion = f32[8,128,8]{2,1,0:T(8,128)S(1)} fusion(f32[8,128,8,128]{3,1,2,0:T(8,128)S(1)} %fusion.23, bf16[8,128,4,8,128]{4,3,2,1,0:T(8,128)(2,1)} %bitcast.74), kind=kLoop, calls=%fused_computation.21 | loop fusion | flops 3137536 | bytes 6324224
  183.6 29.6 %all-to-all-done.1 = bf16[8,1,1,128,2048]{3,4,2,1,0:T(8,128)(2,1)} async-done(((bf16[8,1,1,128,2048]{3,4,2,1,0:T(8,128)(2,1)}), bf16[8,1,1,128,2048]{3,4,2,1,0:T(8,128)(2,1)}, u32[]{:S(2)}, u32[]{:S(2)}) %all-to-all-start.1) | async-done | bytes 4194336 | tf_op jit(solution)/shard_map/all_to_all | solution.py:12
  213.2 4.6 %fusion.50 = (bf16[8,128,1024]{1,2,0:T(8,128)(2,1)}, bf16[8,128,1024]{1,2,0:T(8,128)(2,1)}) fusion(bf16[8,128,2048]{1,2,0:T(8,128)(2,1)} %bitcast.22), kind=kLoop, calls=%fused_computation.116 | loop fusion | bytes 8388608 | tf_op jit(solution)/shard_map/slice | solution.py:28
  217.8 8.2 %fusion.52 = (f32[8,128]{1,0:T(8,128)S(1)}, f32[8,128,8,128]{1,3,2,0:T(8,128)}) fusion(bf16[8,128,1,8,128]{1,4,3,0,2:T(8,128)(2,1)} %copy.35, f32[8,128,8]{1,2,0:T(8,128)S(1)} %multiply_divide_fusion, bf16[8,128,8,128]{1,3,2,0:T(8,128)(2,1)} %bitcast.80, bf16[8,128,8,128]{1,3,2,0:T(8,128)(2,1)} %bitcast.79, f32[8,128]{1,0:T(8,128)S(1)} %fusion.41, ...), kind=kOutput, calls=%fused_computation.118 | convolution fusion | flops 549452800 | bytes 12623904 | tf_op jit(solution)/shard_map/bhij,bjhe->bihe/dot_general | solution.py:40
  226.0 5.4 %copy.27 = f32[8,128,8,128]{3,2,1,0:T(8,128)} copy(f32[8,128,8,128]{1,3,2,0:T(8,128)} %get-tuple-element.48) | data formatting | bytes 8388608 | tf_op jit(solution)/shard_map/add | solution.py:132
  231.4 2.8 %multiply_reduce_fusion.1 = f32[8,128]{1,0:T(8,128)S(1)} fusion(f32[8,128,8,128]{1,3,2,0:T(8,128)} %get-tuple-element.48, f32[8,128]{1,0:T(8,128)S(1)} %get-tuple-element.44), kind=kLoop, calls=%fused_computation.22 | loop fusion | flops 3144704 | bytes 4202496 | tf_op jit(solution)/shard_map/reduce_sum | solution.py:20
  234.3 6.8 %fusion.13 = bf16[1,1,1024,1024]{3,2,1,0:T(8,128)(2,1)} fusion(bf16[1024,1024]{1,0:T(8,128)(2,1)S(1)} %copy-done, f32[128,8,8,128]{3,2,1,0:T(8,128)} %bitcast.78, bf16[1024,4096]{1,0:T(8,128)(2,1)} %multiply_convert_fusion, f32[1024]{0:T(1024)S(1)} %rsqrt_bitcast_fusion, f32[1024]{0:T(1024)S(1)} %get-tuple-element.43, bf16[1024,1024]{1,0:T(8,128)(2,1)S(1)} %copy-done.3, ...), kind=kOutput, calls=%fused_computation.34 | convolution fusion | flops 2156920832 | bytes 12592128 | tf_op jit(solution)/shard_map/dot_general | solution.py:135
  (59 shorter events, 22.2 us)
Async XLA Ops:
  0.0 234.2 %copy-start = (bf16[1024,1024]{1,0:T(8,128)(2,1)S(1)}, bf16[1024,1024]{1,0:T(8,128)(2,1)}, u32[]{:S(2)}) copy-start(bf16[1024,1024]{1,0:T(8,128)(2,1)} %param.21) | copy-start | bytes 6291460
  0.0 11.6 %copy-start.1 = (bf16[1,1,256,1024]{3,2,1,0:T(8,128)(2,1)S(1)}, bf16[1,1,256,1024]{3,2,1,0:T(8,128)(2,1)}, u32[]{:S(2)}) copy-start(bf16[1,1,256,1024]{3,2,1,0:T(8,128)(2,1)} %param.14) | copy-start | bytes 1572868
  0.9 20.6 %collective-permute-start.1 = (s32[3,1024]{1,0:T(4,128)S(1)}, s32[3,1024]{1,0:T(4,128)S(1)}, u32[]{:S(2)}, u32[]{:S(2)}) collective-permute-start(s32[3,1024]{1,0:T(4,128)S(1)} %pad_add_fusion), channel_id=1, source_target_pairs={{0,128},{128,0},{1,129},{129,1},{2,130},{130,2},{3,131},{131,3},{4... | collective-permute-start | bytes 36872 | tf_op jit(solution)/shard_map/ppermute | solution.py:84
  1.5 29.3 %collective-permute-start = (bf16[256,1024]{1,0:T(8,128)(2,1)}, bf16[256,1024]{1,0:T(8,128)(2,1)S(1)}, u32[]{:S(2)}, u32[]{:S(2)}) collective-permute-start(bf16[256,1024]{1,0:T(8,128)(2,1)} %bitcast.70), channel_id=1, source_target_pairs={{0,128},{128,0},{1,129},{129,1},{2,130},{130,2},{3,131},{131,3},{4... | collective-permute-start | bytes 1572872 | tf_op jit(solution)/shard_map/ppermute | solution.py:83
  16.9 3.2 %copy-start.7 = (s32[3]{0:T(128)S(1)}, s32[3]{0:T(128)}, u32[]{:S(2)}) copy-start(s32[3]{0:T(128)} %constant.161.clone.1) | copy-start | bytes 40
  36.1 2.2 copy-start.4
  40.7 7.3 %copy-start.5 = (bf16[1,1,128,2048]{3,2,1,0:T(8,128)(2,1)S(1)}, bf16[1,1,128,2048]{3,2,1,0:T(8,128)(2,1)}, u32[]{:S(2)}) copy-start(bf16[1,1,128,2048]{3,2,1,0:T(8,128)(2,1)} %param.18) | copy-start | bytes 1572868
  40.7 7.5 %copy-start.6 = (s32[1,8]{1,0:T(1,128)S(1)}, s32[1,8]{1,0:T(1,128)}, u32[]{:S(2)}) copy-start(s32[1,8]{1,0:T(1,128)} %param.19) | copy-start | bytes 100
  40.7 75.1 %all-to-all-start = ((bf16[16,136,1024]{2,1,0:T(8,128)(2,1)}), bf16[16,136,1024]{2,1,0:T(8,128)(2,1)}, u32[]{:S(2)}, u32[]{:S(2)}) async-start(bf16[16,136,1024]{2,1,0:T(8,128)(2,1)} %pad_maximum_fusion), calls=%async_computation | async-start | bytes 8912896 | tf_op jit(solution)/shard_map/all_to_all | solution.py:98
  118.3 94.9 %all-to-all-start.1 = ((bf16[8,1,1,128,2048]{3,4,2,1,0:T(8,128)(2,1)}), bf16[8,1,1,128,2048]{3,4,2,1,0:T(8,128)(2,1)}, u32[]{:S(2)}, u32[]{:S(2)}) async-start(bf16[8,1,1,128,2048]{3,4,2,1,0:T(8,128)(2,1)} %stack.5), calls=%async_computation.1 | async-start | bytes 8388608 | tf_op jit(solution)/shard_map/all_to_all | solution.py:12
  138.3 4.8 %copy-start.2 = (bf16[1024,1024]{1,0:T(8,128)(2,1)S(1)}, bf16[1024,1024]{1,0:T(8,128)(2,1)}, u32[]{:S(2)}) copy-start(bf16[1024,1024]{1,0:T(8,128)(2,1)} %gather_fusion) | copy-start | bytes 6291460
  231.4 2.9 %copy-start.3 = (bf16[1024,1024]{1,0:T(8,128)(2,1)S(1)}, bf16[1024,1024]{1,0:T(8,128)(2,1)}, u32[]{:S(2)}) copy-start(bf16[1024,1024]{1,0:T(8,128)(2,1)} %gather_fusion) | copy-start | bytes 6291460
